TPU v7x, 512 devices: a whole 4x4x16 slice. The times are simulated.
512 devices in a mesh: lon: 32 (over z, x_hi), lat: 16 (over x_lo, y, core).
Axes of the slice: x: 4 (x_hi: 2, x_lo: 2; x = x_hi * 2 + x_lo), y: 4, z: 16, core: 2. Of those that a mesh axis runs over, the one named last changes fastest.
Arguments:
- elevation: float32 [12, 1536, 4096], P(None, 'lat', 'lon'), may hold values from -6 to 6
- equilibrium: float32 [12, 1536, 4096], P(None, 'lat', 'lon'), may hold values from -4 to 4
- transport_u: float32 [12, 1536, 4096], P(None, 'lat', 'lon'), may hold values from -4 to 4
- transport_v: float32 [12, 1536, 4096], P(None, 'lat', 'lon'), may hold values from -4 to 4
- ocean_depth: float32 [1536, 4096], P('lat', 'lon'), may hold values from 0.3 to 3
- bottom_drag: float32 [1536, 4096], P('lat', 'lon'), may hold values from 0.2 to 2
- wet_mask: int32 [1536, 4096], P('lat', 'lon'), may hold values 0 or 1
- lon_green: float32 [4096, 128], P('lon'), may hold values from -0.5 to 0.5
- lat_green: float32 [1536, 49152], P('lat', 'lon'), may hold values from -0.0546875 to 0.0546875
Outputs:
- elevation_next: float32 [12, 1536, 4096], P(None, 'lat', 'lon')
- transport_u_next: float32 [12, 1536, 4096], P(None, 'lat', 'lon')
- transport_v_next: float32 [12, 1536, 4096], P(None, 'lat', 'lon')
All inputs are finite; a program needn't handle non-finite values. No bound on the sum of `wet_mask` on one device may be relied on, other than what follows from the above.
Results may differ from a plain program's by a relative error of at most 0.0001.
Values sent between devices are 32-bit elements; how exact they have to be, the bound alone decides.
No kernel may reach another device: no remote copies, remote signals or barrier semaphores. Data moves between devices by JAX's collectives and lax.ppermute only.
A program may use at most 64 MiB of HBM per device.

v0:
```python
import math
import jax
import jax.numpy as jnp
from jax import lax
from jax.sharding import Mesh
from jax.sharding import PartitionSpec as P

FREQS = [1.9323, 2.0, 1.896, 2.0055, 1.0027, 0.9295]
VISCOSITY = 0.5
HALO = 3
LAT = ("chip", "core")


def lat_index():
    return lax.axis_index("chip") * lax.axis_size("core") + lax.axis_index("core")


def lat_size():
    return lax.axis_size("chip") * lax.axis_size("core")


def widen_lon(array, width, dim):
    size, length = (lax.axis_size("lon"), array.shape[dim])
    up = [(i, (i + 1) % size) for i in range(size)]
    down = [(j, i) for i, j in up]
    last = lax.slice_in_dim(array, length - width, length, axis=dim)
    initial = lax.slice_in_dim(array, 0, width, axis=dim)
    before = lax.ppermute(last, "lon", up)
    after = lax.ppermute(initial, "lon", down)
    return jnp.concatenate([before, array, after], axis=dim)


def widen_lat(array, width, dim):
    size, length = (lat_size(), array.shape[dim])
    up = [(i, i + 1) for i in range(size - 1)]
    down = [(j, i) for i, j in up]
    last = lax.slice_in_dim(array, length - width, length, axis=dim)
    initial = lax.slice_in_dim(array, 0, width, axis=dim)
    before = lax.ppermute(last, LAT, up)
    after = lax.ppermute(initial, LAT, down)
    return jnp.concatenate([before, array, after], axis=dim)


def row_terms(rows, nlat):
    angle = (-80.0 + 160.0 * (rows.astype(jnp.float32) + 0.5) / nlat) * (math.pi / 180.0)
    return ((1.0 / jnp.cos(angle))[:, None], (2.0 * jnp.sin(angle))[:, None])


def slopes(potential_ext, stretch):
    east_slope = (potential_ext[:, 1:-1, 2:] - potential_ext[:, 1:-1, :-2]) * 0.5 * stretch
    north_slope = (potential_ext[:, 2:, 1:-1] - potential_ext[:, :-2, 1:-1]) * 0.5
    return (east_slope, north_slope)


def solve_cells(push_u, push_v, drag_field, wet_frac, coriolis):
    damping = drag_field + 4.0 * VISCOSITY
    frequency = jnp.array(FREQS, jnp.float32)[:, None, None]
    det_real = damping * damping - frequency * frequency + coriolis * coriolis
    det_imag = 2.0 * damping * frequency
    magnitude = det_real * det_real + det_imag * det_imag

    def combine(first, second, factor):
        top_real = damping * first[:6] - frequency * first[6:] + factor * coriolis * second[:6]
        top_imag = damping * first[6:] + frequency * first[:6] + factor * coriolis * second[6:]
        out_real = (top_real * det_real + top_imag * det_imag) / magnitude
        out_imag = (top_imag * det_real - top_real * det_imag) / magnitude
        return wet_frac * jnp.concatenate([out_real, out_imag], axis=0)

    return jnp.concatenate([combine(push_u, push_v, 1.0), combine(push_v, push_u, -1.0)], axis=0)


def inner(field, trim):
    return field[..., trim : field.shape[-2] - trim, trim : field.shape[-1] - trim]


def relax(flow_ext, east_slope, north_slope, depth_field, drag_field, wet_frac, coriolis):
    beside_all = (
        flow_ext[:, :-2, 1:-1]
        + flow_ext[:, 2:, 1:-1]
        + flow_ext[:, 1:-1, :-2]
        + flow_ext[:, 1:-1, 2:]
    )
    push_u = -depth_field * east_slope + VISCOSITY * beside_all[:12]
    push_v = -depth_field * north_slope + VISCOSITY * beside_all[12:]
    return solve_cells(push_u, push_v, drag_field, wet_frac, coriolis)


def surface(east_ext, north_ext, stretch, wet_frac):
    spread = (east_ext[:, :, 2:] - east_ext[:, :, :-2]) * 0.5 * stretch + (
        north_ext[:, 2:, :] - north_ext[:, :-2, :]
    ) * 0.5
    frequency = jnp.array(FREQS, jnp.float32)[:, None, None]
    return wet_frac * jnp.concatenate([-spread[6:] / frequency, spread[:6] / frequency], axis=0)


def per_device(
    elevation,
    equilibrium,
    transport_u,
    transport_v,
    ocean_depth,
    bottom_drag,
    wet_mask,
    lon_green,
    lat_green,
):
    rows_here = elevation.shape[1]
    total_rows = rows_here * lat_size()
    wet_frac = wet_mask.astype(jnp.float32)
    source = wet_frac * elevation
    mixed = jnp.einsum("krj,cj->krc", source, lon_green, precision=lax.Precision.HIGHEST)
    columns = mixed.shape[2]
    edge_rows = jnp.concatenate([lon_green[:HALO], lon_green[columns - HALO :]], axis=0)
    edges = jnp.einsum("ej,krj->ker", edge_rows, source, precision=lax.Precision.HIGHEST)
    spare = 8 * ((2 * HALO + 7) // 8)
    edges = jnp.pad(edges, ((0, 0), (0, spare - 2 * HALO), (0, columns - rows_here)))
    packed = jnp.concatenate([mixed, edges], axis=1)
    gathered = lax.all_gather(packed, LAT, axis=1, tiled=True)
    fields = jnp.stack([ocean_depth, bottom_drag, wet_frac], axis=0)
    stack = jnp.concatenate([elevation - equilibrium, transport_u, transport_v, fields], axis=0)
    stack = widen_lat(widen_lon(stack, HALO, 2), HALO, 1)
    green_ext = widen_lat(lat_green, HALO, 0)
    blocks = lat_size()
    block = rows_here + spare
    green_blocks = green_ext.reshape(green_ext.shape[0], blocks, rows_here)
    lanes = gathered.reshape(12, blocks, block, columns)[
        :, :, rows_here : rows_here + 2 * HALO, :rows_here
    ]
    edge_sal = jnp.einsum("rbj,kbej->kre", green_blocks, lanes, precision=lax.Precision.HIGHEST)
    size = lax.axis_size("lon")
    up = [(i, (i + 1) % size) for i in range(size)]
    down = [(j, i) for i, j in up]
    before = lax.ppermute(edge_sal[:, :, HALO:], "lon", up)
    after = lax.ppermute(edge_sal[:, :, :HALO], "lon", down)
    green_pad = jnp.pad(green_blocks, ((0, 0), (0, 0), (0, spare))).reshape(green_ext.shape[0], -1)
    sal = jnp.einsum("rs,ksc->krc", green_pad, gathered, precision=lax.Precision.HIGHEST)
    sal = jnp.concatenate([before, sal, after], axis=2)
    potential = stack[:12] - sal
    flows = stack[12:36]
    depth_ext, drag_ext, wet_ext = (stack[36], stack[37], stack[38])
    first_row = lat_index() * rows_here - HALO
    stretch, coriolis = row_terms(first_row + jnp.arange(rows_here + 2 * HALO), total_rows)
    east_slope, north_slope = slopes(potential, stretch[1:-1])
    flows = relax(
        flows,
        east_slope,
        north_slope,
        inner(depth_ext, 1),
        inner(drag_ext, 1),
        inner(wet_ext, 1),
        coriolis[1:-1],
    )
    flows = relax(
        flows,
        inner(east_slope, 1),
        inner(north_slope, 1),
        inner(depth_ext, 2),
        inner(drag_ext, 2),
        inner(wet_ext, 2),
        coriolis[2:-2],
    )
    east_ext = flows[:12, 1:-1, :]
    north_ext = flows[12:, :, 1:-1]
    elevation_next = surface(east_ext, north_ext, stretch[HALO:-HALO], wet_frac)
    flows = inner(flows, 1)
    return (elevation_next, flows[:12], flows[12:])


def solution(mesh):
    lat_devices = mesh.shape["lat"]
    cores = 2 if lat_devices % 2 == 0 else 1
    devices = mesh.devices.reshape(mesh.shape["lon"], lat_devices // cores, cores)
    split = Mesh(devices, ("lon", "chip", "core"))
    grid = P(None, LAT, "lon")
    plane = P(LAT, "lon")
    placed = (grid, grid, grid, grid, plane, plane, plane, P("lon", None), plane)
    return jax.shard_map(
        per_device, mesh=split, in_specs=placed, out_specs=(grid, grid, grid), check_vma=False
    )
```

profile of v0, /device:TPU:1, one launch (start us, length us, event | category | flops | bytes accessed | tf_op | source)
XLA Modules:
  0.0 135.8 jit_solution(12874723545811327905)
XLA Ops:
  12.7 4.6 %collective-permute-start.4 = (f32[3,1536]{1,0:T(4,128)S(1)}, f32[3,1536]{1,0:T(4,128)S(1)}, u32[]{:S(2)}, u32[]{:S(2)}) collective-permute-start(f32[3,1536]{1,0:T(4,128)S(1)} %get-tuple-element.41), channel_id=1, source_target_pairs={{0,1},{1,2},{2,3},{3,4},{4,5},{5,6},{6,7},{7,8},{8,9},{9,10},{10,1... | collective-permute-start | bytes 55304 | tf_op jit(solution)/shard_map/ppermute | solution.py:39
  17.3 5.6 %collective-permute-start.5 = (f32[3,1536]{1,0:T(4,128)S(1)}, f32[3,1536]{1,0:T(4,128)S(1)}, u32[]{:S(2)}, u32[]{:S(2)}) collective-permute-start(f32[3,1536]{1,0:T(4,128)S(1)} %get-tuple-element.42), channel_id=1, source_target_pairs={{1,0},{2,1},{3,2},{4,3},{5,4},{6,5},{7,6},{8,7},{9,8},{10,9},{11,1... | collective-permute-start | bytes 55304 | tf_op jit(solution)/shard_map/ppermute | solution.py:40
  25.4 2.6 %fusion.57 = (f32[39,96,3]{2,1,0:T(8,128)}, f32[39,96,3]{2,1,0:T(8,128)}) fusion(f32[39,96,128]{2,1,0:T(8,128)S(1)} %bitcast_dynamic-update-slice_fusion), kind=kLoop, calls=%fused_computation.140 | loop fusion | bytes 179712 | tf_op jit(solution)/shard_map/slice | solution.py:26
  28.0 2.1 %copy.21 = f32[39,96,3]{1,0,2:T(8,128)S(1)} copy(f32[39,96,3]{2,1,0:T(8,128)} %get-tuple-element.35) | data formatting | bytes 89856 | tf_op jit(solution)/shard_map/slice | solution.py:27
  30.1 10.0 %collective-permute-start.1 = (f32[39,96,3]{1,0,2:T(8,128)S(1)}, f32[39,96,3]{1,0,2:T(8,128)S(1)}, u32[]{:S(2)}, u32[]{:S(2)}) collective-permute-start(f32[39,96,3]{1,0,2:T(8,128)S(1)} %copy.21), channel_id=1, source_target_pairs={{16,0},{32,16},{48,32},{64,48},{80,64},{96,80},{112,96},{128,112},... | collective-permute-start | bytes 134792 | tf_op jit(solution)/shard_map/ppermute | solution.py:29
  40.2 2.1 %copy.20 = f32[39,96,3]{1,0,2:T(8,128)S(1)} copy(f32[39,96,3]{2,1,0:T(8,128)} %get-tuple-element.34) | data formatting | bytes 89856 | tf_op jit(solution)/shard_map/slice | solution.py:26
  42.3 1.9 %collective-permute-start = (f32[39,96,3]{1,0,2:T(8,128)S(1)}, f32[39,96,3]{1,0,2:T(8,128)S(1)}, u32[]{:S(2)}, u32[]{:S(2)}) collective-permute-start(f32[39,96,3]{1,0,2:T(8,128)S(1)} %copy.20), channel_id=1, source_target_pairs={{0,16},{16,32},{32,48},{48,64},{64,80},{80,96},{96,112},{112,128},... | collective-permute-start | bytes 134792 | tf_op jit(solution)/shard_map/ppermute | solution.py:28
  47.0 4.0 %collective-permute-done = f32[39,96,3]{1,0,2:T(8,128)S(1)} collective-permute-done((f32[39,96,3]{1,0,2:T(8,128)S(1)}, f32[39,96,3]{1,0,2:T(8,128)S(1)}, u32[]{:S(2)}, u32[]{:S(2)}) %collective-permute-start) | collective-permute-done | bytes 44960 | tf_op jit(solution)/shard_map/ppermute | solution.py:28
  51.0 1.9 %copy.22 = f32[39,96,3]{2,1,0:T(8,128)} copy(f32[39,96,3]{1,0,2:T(8,128)S(1)} %collective-permute-done) | data formatting | bytes 89856 | tf_op jit(solution)/shard_map/ppermute | solution.py:28
  52.9 1.9 %copy.23 = f32[39,96,3]{2,1,0:T(8,128)} copy(f32[39,96,3]{1,0,2:T(8,128)S(1)} %collective-permute-done.1) | data formatting | bytes 89856 | tf_op jit(solution)/shard_map/ppermute | solution.py:29
  54.8 2.2 %pad_maximum_fusion.5 = (f32[39,3,134]{2,1,0:T(4,128)}, f32[39,3,134]{2,1,0:T(4,128)}) fusion(f32[39,96,3]{2,1,0:T(8,128)} %copy.23, f32[39,96,128]{2,1,0:T(8,128)S(1)} %bitcast_dynamic-update-slice_fusion, f32[39,96,3]{2,1,0:T(8,128)} %copy.22), kind=kLoop, calls=%fused_computation.108 | loop fusion | flops 62712 | bytes 2132208 | tf_op jit(solution)/shard_map/slice | solution.py:37
  57.0 5.0 %collective-permute-start.2 = (f32[39,3,134]{2,1,0:T(4,128)}, f32[39,3,134]{2,1,0:T(4,128)S(1)}, u32[]{:S(2)}, u32[]{:S(2)}) collective-permute-start(f32[39,3,134]{2,1,0:T(4,128)} %get-tuple-element.22), channel_id=1, source_target_pairs={{0,1},{1,2},{2,3},{3,4},{4,5},{5,6},{6,7},{7,8},{8,9},{9,10},{10,1... | collective-permute-start | bytes 188144 | tf_op jit(solution)/shard_map/ppermute | solution.py:39
  62.0 1.9 %collective-permute-start.3 = (f32[39,3,134]{2,1,0:T(4,128)}, f32[39,3,134]{2,1,0:T(4,128)}, u32[]{:S(2)}, u32[]{:S(2)}) collective-permute-start(f32[39,3,134]{2,1,0:T(4,128)} %get-tuple-element.23), channel_id=1, source_target_pairs={{1,0},{2,1},{3,2},{4,3},{5,4},{6,5},{7,6},{8,7},{9,8},{10,9},{11,1... | collective-permute-start | bytes 188144 | tf_op jit(solution)/shard_map/ppermute | solution.py:40
  65.3 2.4 %collective-permute-done.2 = f32[39,3,134]{2,1,0:T(4,128)S(1)} collective-permute-done((f32[39,3,134]{2,1,0:T(4,128)}, f32[39,3,134]{2,1,0:T(4,128)S(1)}, u32[]{:S(2)}, u32[]{:S(2)}) %collective-permute-start.2) | collective-permute-done | bytes 62744 | tf_op jit(solution)/shard_map/ppermute | solution.py:39
  67.7 4.9 %collective-permute-done.3 = f32[39,3,134]{2,1,0:T(4,128)} collective-permute-done((f32[39,3,134]{2,1,0:T(4,128)}, f32[39,3,134]{2,1,0:T(4,128)}, u32[]{:S(2)}, u32[]{:S(2)}) %collective-permute-start.3) | collective-permute-done | bytes 62744 | tf_op jit(solution)/shard_map/ppermute | solution.py:40
  75.4 2.6 %pad_maximum_fusion = f32[39,102,134]{2,1,0:T(8,128)S(1)} fusion(f32[39,3,134]{2,1,0:T(4,128)} %collective-permute-done.3, f32[39,96,3]{2,1,0:T(8,128)S(1)} %copy-done.2, f32[39,96,128]{2,1,0:T(8,128)S(1)} %bitcast_dynamic-update-slice_fusion, f32[39,96,3]{2,1,0:T(8,128)S(1)} %copy-done.1, f32[39,3,134]{2,1,0:T(4,128)S(1)} %collective-permute-done.2), kind=kLoop, calls=%fused_computation | loop fusion | flops 2132208 | bytes 4264416 | tf_op jit(solution)/shard_map/concatenate | solution.py:41
  80.9 2.1 %slice_add_fusion = f32[24,100,132]{2,1,0:T(8,128)S(1)} fusion(f32[39,102,134]{2,1,0:T(8,128)S(1)} %pad_maximum_fusion), kind=kLoop, calls=%fused_computation.14 | loop fusion | flops 950400 | bytes 6336000 | tf_op jit(solution)/shard_map/add | solution.py:78
  83.0 7.1 %all-gather.2.cloned.1.call-done = f32[12,1664,128]{2,1,0:T(8,128)} async-done(((f32[12,104,128]{2,1,0:T(8,128)}), f32[12,1664,128]{2,1,0:T(8,128)}) %all-gather.2.cloned.1.call-update) | async-done | bytes 10223632 | tf_op jit(solution)/shard_map/all_gather | solution.py:118
  92.7 4.0 %collective-permute-start.6 = (f32[12,102,3]{1,0,2:T(8,128)S(1)}, f32[12,102,3]{1,0,2:T(8,128)S(1)}, u32[]{:S(2)}, u32[]{:S(2)}) collective-permute-start(f32[12,102,3]{1,0,2:T(8,128)S(1)} %get-tuple-element.61), channel_id=1, source_target_pairs={{0,16},{16,32},{32,48},{48,64},{64,80},{80,96},{96,112},{112,128},... | collective-permute-start | bytes 44072 | tf_op jit(solution)/shard_map/ppermute | solution.py:133
  96.7 6.9 %collective-permute-start.7 = (f32[12,102,3]{1,0,2:T(8,128)S(1)}, f32[12,102,3]{1,0,2:T(8,128)S(1)}, u32[]{:S(2)}, u32[]{:S(2)}) collective-permute-start(f32[12,102,3]{1,0,2:T(8,128)S(1)} %get-tuple-element.62), channel_id=1, source_target_pairs={{16,0},{32,16},{48,32},{64,48},{80,64},{96,80},{112,96},{128,112},... | collective-permute-start | bytes 44072 | tf_op jit(solution)/shard_map/ppermute | solution.py:134
  103.6 9.3 %convolution_bitcast_fusion = f32[12,102,128]{2,1,0:T(8,128)S(1)} fusion(f32[12,1664,128]{2,1,0:T(8,128)} %all-gather.2.cloned.1.call-done, f32[102,1664,1]{0,1,2:T(8,128)S(1)} %bitcast.40), kind=kOutput, calls=%fused_computation.46 | convolution fusion | flops 3128426496 | bytes 11529216 | tf_op jit(solution)/shard_map/rs,ksc->krc/dot_general | solution.py:136
  115.3 2.3 %slice_subtract_fusion.2 = f32[12,102,134]{2,1,0:T(8,128)S(1)} fusion(f32[39,102,134]{2,1,0:T(8,128)} %copy-done, f32[12,102,3]{2,1,0:T(8,128)} %copy.28, f32[12,102,128]{2,1,0:T(8,128)S(1)} %convolution_bitcast_fusion, f32[12,102,3]{2,1,0:T(8,128)} %copy.27), kind=kLoop, calls=%fused_computation.41 | loop fusion | flops 492048 | bytes 1968192 | tf_op jit(solution)/shard_map/sub | solution.py:138
  120.7 2.1 %fusion.2 = f32[24,98,130]{2,1,0:T(8,128)S(1)} fusion(f32[12,100,132]{2,1,0:T(8,128)S(1)} %get-tuple-element.53, f32[12,100,132]{2,1,0:T(8,128)S(1)} %get-tuple-element.52), kind=kLoop, calls=%fused_computation.9 | loop fusion | flops 2140320 | bytes 2490240 | tf_op jit(solution)/shard_map/add | solution.py:78
  126.1 1.8 %fusion.58 = (f32[12,96,128]{2,1,0:T(8,128)}, f32[12,96,128]{2,1,0:T(8,128)S(1)}, f32[12,96,128]{2,1,0:T(8,128)}) fusion(f32[12,98,130]{2,1,0:T(8,128)S(1)} %get-tuple-element.48, f32[96]{0:T(128)S(1)} %copy-done.30, f32[12,98,130]{2,1,0:T(8,128)S(1)} %get-tuple-element.47), kind=kLoop, calls=%fused_computation.141 | loop fusion | flops 737280 | bytes 5308800 | tf_op jit(solution)/shard_map/slice | solution.py:166
  (113 shorter events, 29.6 us)
Async XLA Ops:
  7.2 3.4 %copy-start.3 = (f32[12,96,128]{2,1,0:T(8,128)S(1)}, f32[12,96,128]{2,1,0:T(8,128)}, u32[]{:S(2)}) copy-start(f32[12,96,128]{2,1,0:T(8,128)} %param.12) | copy-start | bytes 1769476
  7.2 83.0 %all-gather.2.cloned.1.call-start = ((), (), s32[]{:S(2)}) async-start(), calls=%async_computation | async-start | bytes 10862592 | tf_op jit(solution)/shard_map/all_gather | solution.py:118
  8.8 1.7 %copy-start.7 = (f32[96,128]{1,0:T(8,128)}, f32[96,128]{1,0:T(8,128)S(1)}, u32[]{:S(2)}) copy-start(f32[96,128]{1,0:T(8,128)S(1)} %convert_element_type.10) | copy-start | bytes 147460
  10.5 2.1 %copy-start.9 = (f32[96,1536]{1,0:T(8,128)S(1)}, f32[96,1536]{1,0:T(8,128)}, u32[]{:S(2)}) copy-start(f32[96,1536]{1,0:T(8,128)} %param.20) | copy-start | bytes 1769476
  12.7 51.2 %collective-permute-start.4 = (f32[3,1536]{1,0:T(4,128)S(1)}, f32[3,1536]{1,0:T(4,128)S(1)}, u32[]{:S(2)}, u32[]{:S(2)}) collective-permute-start(f32[3,1536]{1,0:T(4,128)S(1)} %get-tuple-element.41), channel_id=1, source_target_pairs={{0,1},{1,2},{2,3},{3,4},{4,5},{5,6},{6,7},{7,8},{8,9},{9,10},{10,1... | collective-permute-start | bytes 55304 | tf_op jit(solution)/shard_map/ppermute | solution.py:39
  17.3 7.9 %copy-start.10 = (f32[12,96,128]{2,1,0:T(8,128)S(1)}, f32[12,96,128]{2,1,0:T(8,128)}, u32[]{:S(2)}) copy-start(f32[12,96,128]{2,1,0:T(8,128)} %param.15) | copy-start | bytes 1769476
  17.3 46.6 %collective-permute-start.5 = (f32[3,1536]{1,0:T(4,128)S(1)}, f32[3,1536]{1,0:T(4,128)S(1)}, u32[]{:S(2)}, u32[]{:S(2)}) collective-permute-start(f32[3,1536]{1,0:T(4,128)S(1)} %get-tuple-element.42), channel_id=1, source_target_pairs={{1,0},{2,1},{3,2},{4,3},{5,4},{6,5},{7,6},{8,7},{9,8},{10,9},{11,1... | collective-permute-start | bytes 55304 | tf_op jit(solution)/shard_map/ppermute | solution.py:40
  24.1 1.3 copy-start.18
  30.1 22.7 %collective-permute-start.1 = (f32[39,96,3]{1,0,2:T(8,128)S(1)}, f32[39,96,3]{1,0,2:T(8,128)S(1)}, u32[]{:S(2)}, u32[]{:S(2)}) collective-permute-start(f32[39,96,3]{1,0,2:T(8,128)S(1)} %copy.21), channel_id=1, source_target_pairs={{16,0},{32,16},{48,32},{64,48},{80,64},{96,80},{112,96},{128,112},... | collective-permute-start | bytes 134792 | tf_op jit(solution)/shard_map/ppermute | solution.py:29
  42.3 8.7 %collective-permute-start = (f32[39,96,3]{1,0,2:T(8,128)S(1)}, f32[39,96,3]{1,0,2:T(8,128)S(1)}, u32[]{:S(2)}, u32[]{:S(2)}) collective-permute-start(f32[39,96,3]{1,0,2:T(8,128)S(1)} %copy.20), channel_id=1, source_target_pairs={{0,16},{16,32},{32,48},{48,64},{64,80},{80,96},{96,112},{112,128},... | collective-permute-start | bytes 134792 | tf_op jit(solution)/shard_map/ppermute | solution.py:28
  57.0 10.7 %collective-permute-start.2 = (f32[39,3,134]{2,1,0:T(4,128)}, f32[39,3,134]{2,1,0:T(4,128)S(1)}, u32[]{:S(2)}, u32[]{:S(2)}) collective-permute-start(f32[39,3,134]{2,1,0:T(4,128)} %get-tuple-element.22), channel_id=1, source_target_pairs={{0,1},{1,2},{2,3},{3,4},{4,5},{5,6},{6,7},{7,8},{8,9},{9,10},{10,1... | collective-permute-start | bytes 188144 | tf_op jit(solution)/shard_map/ppermute | solution.py:39
  62.0 10.6 %collective-permute-start.3 = (f32[39,3,134]{2,1,0:T(4,128)}, f32[39,3,134]{2,1,0:T(4,128)}, u32[]{:S(2)}, u32[]{:S(2)}) collective-permute-start(f32[39,3,134]{2,1,0:T(4,128)} %get-tuple-element.23), channel_id=1, source_target_pairs={{1,0},{2,1},{3,2},{4,3},{5,4},{6,5},{7,6},{8,7},{9,8},{10,9},{11,1... | collective-permute-start | bytes 188144 | tf_op jit(solution)/shard_map/ppermute | solution.py:40
  72.6 2.8 %copy-start.1 = (f32[39,96,3]{2,1,0:T(8,128)S(1)}, f32[39,96,3]{2,1,0:T(8,128)}, u32[]{:S(2)}) copy-start(f32[39,96,3]{2,1,0:T(8,128)} %copy.22) | copy-start | bytes 134788
  72.6 2.8 %copy-start.2 = (f32[39,96,3]{2,1,0:T(8,128)S(1)}, f32[39,96,3]{2,1,0:T(8,128)}, u32[]{:S(2)}) copy-start(f32[39,96,3]{2,1,0:T(8,128)} %copy.23) | copy-start | bytes 134788
  78.0 2.9 %copy-start = (f32[39,102,134]{2,1,0:T(8,128)}, f32[39,102,134]{2,1,0:T(8,128)S(1)}, u32[]{:S(2)}) copy-start(f32[39,102,134]{2,1,0:T(8,128)S(1)} %pad_maximum_fusion) | copy-start | bytes 6396628
  90.2 13.4 %copy-start.4 = (f32[102,16,104]{0,2,1:T(8,128)S(1)}, f32[102,16,104]{0,2,1:T(8,128)}, u32[]{:S(2)}) copy-start(f32[102,16,104]{0,2,1:T(8,128)} %pad.9) | copy-start | bytes 2036740
  92.7 21.4 %collective-permute-start.6 = (f32[12,102,3]{1,0,2:T(8,128)S(1)}, f32[12,102,3]{1,0,2:T(8,128)S(1)}, u32[]{:S(2)}, u32[]{:S(2)}) collective-permute-start(f32[12,102,3]{1,0,2:T(8,128)S(1)} %get-tuple-element.61), channel_id=1, source_target_pairs={{0,16},{16,32},{32,48},{48,64},{64,80},{80,96},{96,112},{112,128},... | collective-permute-start | bytes 44072 | tf_op jit(solution)/shard_map/ppermute | solution.py:133
  96.7 16.3 %collective-permute-start.7 = (f32[12,102,3]{1,0,2:T(8,128)S(1)}, f32[12,102,3]{1,0,2:T(8,128)S(1)}, u32[]{:S(2)}, u32[]{:S(2)}) collective-permute-start(f32[12,102,3]{1,0,2:T(8,128)S(1)} %get-tuple-element.62), channel_id=1, source_target_pairs={{16,0},{32,16},{48,32},{64,48},{80,64},{96,80},{112,96},{128,112},... | collective-permute-start | bytes 44072 | tf_op jit(solution)/shard_map/ppermute | solution.py:134
  115.2 2.3 %copy-start.12 = (f32[100,132]{1,0:T(8,128)S(1)}, f32[100,132]{1,0:T(8,128)}, u32[]{:S(2)}) copy-start(f32[100,132]{1,0:T(8,128)} %get-tuple-element.57) | copy-start | bytes 158404
  115.2 2.3 %copy-start.13 = (f32[100,132]{1,0:T(8,128)S(1)}, f32[100,132]{1,0:T(8,128)}, u32[]{:S(2)}) copy-start(f32[100,132]{1,0:T(8,128)} %get-tuple-element.58) | copy-start | bytes 158404
  115.2 2.3 %copy-start.31 = (f32[100]{0:T(128)S(1)}, f32[100]{0:T(128)}, u32[]{:S(2)}) copy-start(f32[100]{0:T(128)} %slice_multiply_fusion.8) | copy-start | bytes 1204
  120.7 2.1 %copy-start.11 = (f32[98,130]{1,0:T(8,128)S(1)}, f32[98,130]{1,0:T(8,128)}, u32[]{:S(2)}) copy-start(f32[98,130]{1,0:T(8,128)} %get-tuple-element.69) | copy-start | bytes 152884
  126.1 1.9 %copy-start.29 = (f32[6]{0:T(128)S(1)}, f32[6]{0:T(128)}, u32[]{:S(2)}) copy-start(f32[6]{0:T(128)} %constant.48) | copy-start | bytes 76
  126.1 2.0 %copy-start.8 = (f32[96,128]{1,0:T(8,128)S(1)}, f32[96,128]{1,0:T(8,128)}, u32[]{:S(2)}) copy-start(f32[96,128]{1,0:T(8,128)} %copy-done.7) | copy-start | bytes 147460
  (17 other events, 18.1 us)
Sparse Core Ops, SparseCore 0:
  12.8 77.3 all-gather.1
where the time goes:
time: 137 us; the launch traced here: 136 us
  starting transfers between devices  40 us (29%)
  other arithmetic  28.6 us (21%)
  local copies, waits for them, and re-layouts  20.5 us (15%)
  waiting for transfers between devices  18.5 us (14%)
  between operations  14.7 us (11%)
  matrix products  13.5 us (10%)
    ppermute x1, starting transfers between devices, widen_lon(): after = lax.ppermute(initial, 'lon', down)  10 us
    ppermute x2, starting transfers between devices, widen_lat(): before = lax.ppermute(last, LAT, up)  9.59 us
    dot_general x1, matrix products, per_device(): jnp.einsum('rs,ksc->krc', green_pad, gathered, precision=lax.Precision.HI...  9.34 us
    ppermute x2, starting transfers between devices, widen_lat(): after = lax.ppermute(initial, LAT, down)  7.52 us
    all_gather x1, waiting for transfers between devices, per_device(): gathered = lax.all_gather(packed, LAT, axis=1, tiled=True)  7.14 us
    ppermute x1, starting transfers between devices, per_device(): after = lax.ppermute(edge_sal[:, :, :HALO], 'lon', down)  6.9 us
    ppermute x2, waiting for transfers between devices, widen_lat(): after = lax.ppermute(initial, LAT, down)  4.93 us
    slice x2, local copies, waits for them, and re-layouts, widen_lon(): last = lax.slice_in_dim(array, length - width, length, axis=dim)  4.77 us
  transfers between devices with their start and end apart: 9, of which 4 were waited for; matrix products, arithmetic and copies ran while one was open for 30% of the time, Pallas kernels for 0%

commit v1 on v0

--- a/solution.py
+++ b/solution.py
@@ -115,7 +115,9 @@
     spare = 8 * ((2 * HALO + 7) // 8)
     edges = jnp.pad(edges, ((0, 0), (0, spare - 2 * HALO), (0, columns - rows_here)))
     packed = jnp.concatenate([mixed, edges], axis=1)
-    gathered = lax.all_gather(packed, LAT, axis=1, tiled=True)
+    gathered = jnp.concatenate(
+        lax.all_to_all(jnp.stack([packed] * lax.axis_size(LAT)), LAT, 0, 0), axis=1
+    )
     fields = jnp.stack([ocean_depth, bottom_drag, wet_frac], axis=0)
     stack = jnp.concatenate([elevation - equilibrium, transport_u, transport_v, fields], axis=0)
     stack = widen_lat(widen_lon(stack, HALO, 2), HALO, 1)

time: 137 us -> 258 us (1.88)
  waiting for transfers between devices: 18.5 us -> 128 us
  local copies, waits for them, and re-layouts: 20.5 us -> 35.5 us
  between operations: 14.7 us -> 1.26 us
  starting transfers between devices: 40 us -> 49.2 us
    ppermute x1, waiting for transfers between devices: 0.01 us -> 126 us  [widen_lon(): after = lax.ppermute(initial, 'lon', down)]
    all_to_all x0 -> x1, starting transfers between devices: none -> 11.6 us  [per_device(): lax.all_to_all(jnp.stack([packed] * lax.axis_size(LAT)), LAT, 0, 0)]
    all_to_all x0 -> x1, local copies, waits for them, and re-layouts: none -> 11 us  [per_device(): lax.all_to_all(jnp.stack([packed] * lax.axis_size(LAT)), LAT, 0, 0)]
    all_gather x1 -> x0, waiting for transfers between devices: 7.14 us -> none  [per_device(): gathered = lax.all_gather(packed, LAT, axis=1, tiled=True)]
    another operation x0 -> x1, local copies, waits for them, and re-layouts: none -> 4.92 us  [per_device(): jnp.stack([packed] * lax.axis_size(LAT))]
    ppermute x2, waiting for transfers between devices: 4.93 us -> 0.65 us  [widen_lat(): after = lax.ppermute(initial, LAT, down)]
    ppermute x1, waiting for transfers between devices: 4 us -> 0.01 us  [widen_lon(): before = lax.ppermute(last, 'lon', up)]
    ppermute x1, starting transfers between devices: 6.9 us -> 10.1 us  [per_device(): after = lax.ppermute(edge_sal[:, :, :HALO], 'lon', down)]
  transfers between devices with their start and end apart: 9 -> 9, of which waited for: 4 -> 3; matrix products, arithmetic and copies ran while one was open for 30% -> 15% of each run, Pallas kernels for 0% -> 0%
where the time goes in v1:
time: 258 us; the launch traced here: 257 us
  waiting for transfers between devices  128 us (50%)
  starting transfers between devices  49.2 us (19%)
  local copies, waits for them, and re-layouts  35.5 us (14%)
  other arithmetic  26.4 us (10%)
  matrix products  16 us (6%)
    ppermute x1, waiting for transfers between devices, widen_lon(): after = lax.ppermute(initial, 'lon', down)  126 us
    all_to_all x1, starting transfers between devices, per_device(): lax.all_to_all(jnp.stack([packed] * lax.axis_size(LAT)), LAT, 0, 0)  11.6 us
    all_to_all x1, local copies, waits for them, and re-layouts, per_device(): lax.all_to_all(jnp.stack([packed] * lax.axis_size(LAT)), LAT, 0, 0)  11 us
    ppermute x1, starting transfers between devices, per_device(): after = lax.ppermute(edge_sal[:, :, :HALO], 'lon', down)  10.1 us
    ppermute x2, starting transfers between devices, widen_lat(): before = lax.ppermute(last, LAT, up)  10.1 us
    dot_general x1, matrix products, per_device(): jnp.einsum('rs,ksc->krc', green_pad, gathered, precision=lax.Precision.HI...  9.86 us
    ppermute x1, starting transfers between devices, widen_lon(): after = lax.ppermute(initial, 'lon', down)  8.75 us
  transfers between devices with their start and end apart: 9, of which 3 were waited for; matrix products, arithmetic and copies ran while one was open for 15% of the time, Pallas kernels for 0%

profile of v1, /device:TPU:1, one launch (start us, length us, event | category | flops | bytes accessed | tf_op | source)
XLA Modules:
  0.0 256.7 jit_solution(11137430548888813602)
XLA Ops:
  3.9 2.2 convolution_bitcast_fusion.1
  6.2 4.9 %stack.8 = f32[16,12,104,128]{3,2,1,0:T(8,128)} broadcast(f32[12,104,128]{2,1,0:T(8,128)S(1)} %select_maximum_fusion), dimensions={1,2,3} | broadcast | bytes 10862592 | tf_op jit(solution)/shard_map/stack | solution.py:119
  11.1 11.6 %all-to-all-start = ((f32[16,12,104,128]{3,2,1,0:T(8,128)}), f32[16,12,104,128]{3,2,1,0:T(8,128)}, u32[]{:S(2)}, u32[]{:S(2)}) async-start(f32[16,12,104,128]{3,2,1,0:T(8,128)} %stack.8), calls=%async_computation | async-start | bytes 20447232 | tf_op jit(solution)/shard_map/all_to_all | solution.py:119
  24.1 2.6 %fusion.65 = (f32[39,96,3]{2,1,0:T(8,128)}, f32[39,96,3]{2,1,0:T(8,128)}) fusion(f32[39,96,128]{2,1,0:T(8,128)S(1)} %bitcast_dynamic-update-slice_fusion), kind=kLoop, calls=%fused_computation.146 | loop fusion | bytes 179712 | tf_op jit(solution)/shard_map/slice | solution.py:26
  26.7 2.2 copy.22
  28.9 8.8 %collective-permute-start.1 = (f32[39,96,3]{1,0,2:T(8,128)S(1)}, f32[39,96,3]{1,0,2:T(8,128)S(1)}, u32[]{:S(2)}, u32[]{:S(2)}) collective-permute-start(f32[39,96,3]{1,0,2:T(8,128)S(1)} %copy.22), channel_id=1, source_target_pairs={{16,0},{32,16},{48,32},{64,48},{80,64},{96,80},{112,96},{128,112},... | collective-permute-start | bytes 134792 | tf_op jit(solution)/shard_map/ppermute | solution.py:29
  37.6 2.1 copy.21
  39.7 1.9 collective-permute-start
  41.7 2.4 collective-permute-start.5
  44.1 3.4 %collective-permute-start.4 = (f32[3,1536]{1,0:T(4,128)S(1)}, f32[3,1536]{1,0:T(4,128)S(1)}, u32[]{:S(2)}, u32[]{:S(2)}) collective-permute-start(f32[3,1536]{1,0:T(4,128)S(1)} %get-tuple-element.41), channel_id=1, source_target_pairs={{0,1},{1,2},{2,3},{3,4},{4,5},{5,6},{6,7},{7,8},{8,9},{9,10},{10,1... | collective-permute-start | bytes 55304 | tf_op jit(solution)/shard_map/ppermute | solution.py:39
  50.1 126.3 %collective-permute-done.1 = f32[39,96,3]{1,0,2:T(8,128)S(1)} collective-permute-done((f32[39,96,3]{1,0,2:T(8,128)S(1)}, f32[39,96,3]{1,0,2:T(8,128)S(1)}, u32[]{:S(2)}, u32[]{:S(2)}) %collective-permute-start.1) | collective-permute-done | bytes 44960 | tf_op jit(solution)/shard_map/ppermute | solution.py:29
  176.4 1.9 copy.24
  178.4 2.0 copy.23
  180.4 2.2 pad_maximum_fusion.5
  182.5 2.5 collective-permute-start.3
  185.0 6.7 %collective-permute-start.2 = (f32[39,3,134]{2,1,0:T(4,128)}, f32[39,3,134]{2,1,0:T(4,128)}, u32[]{:S(2)}, u32[]{:S(2)}) collective-permute-start(f32[39,3,134]{2,1,0:T(4,128)} %get-tuple-element.22), channel_id=1, source_target_pairs={{0,1},{1,2},{2,3},{3,4},{4,5},{5,6},{6,7},{7,8},{8,9},{9,10},{10,1... | collective-permute-start | bytes 188144 | tf_op jit(solution)/shard_map/ppermute | solution.py:39
  196.7 2.6 %pad_maximum_fusion = f32[39,102,134]{2,1,0:T(8,128)S(1)} fusion(f32[39,3,134]{2,1,0:T(4,128)S(1)} %collective-permute-done.3, f32[39,96,3]{2,1,0:T(8,128)S(1)} %copy-done.1, f32[39,96,128]{2,1,0:T(8,128)S(1)} %bitcast_dynamic-update-slice_fusion, f32[39,96,3]{2,1,0:T(8,128)S(1)} %copy-done.2, f32[39,3,134]{2,1,0:T(4,128)} %collective-permute-done.2), kind=kLoop, calls=%fused_computation.3 | loop fusion | flops 2132208 | bytes 4264416 | tf_op jit(solution)/shard_map/concatenate | solution.py:41
  202.3 2.1 slice_add_fusion
  204.4 11.0 %copy.37 = f32[16,12,104,128]{3,1,0,2:T(8,128)} copy(f32[16,12,104,128]{3,2,1,0:T(8,128)} %all-to-all-done) | data formatting | bytes 20447232 | tf_op jit(solution)/shard_map/all_to_all | solution.py:119
  215.4 2.2 convolution_bitcast_fusion
  218.2 10.1 %collective-permute-start.7 = (f32[12,102,3]{1,0,2:T(8,128)S(1)}, f32[12,102,3]{1,0,2:T(8,128)}, u32[]{:S(2)}, u32[]{:S(2)}) collective-permute-start(f32[12,102,3]{1,0,2:T(8,128)S(1)} %get-tuple-element.62), channel_id=1, source_target_pairs={{16,0},{32,16},{48,32},{64,48},{80,64},{96,80},{112,96},{128,112},... | collective-permute-start | bytes 44072 | tf_op jit(solution)/shard_map/ppermute | solution.py:136
  230.2 9.9 %fusion.14 = f32[12,102,128]{2,1,0:T(8,128)} fusion(f32[16,12,104,128]{3,2,1,0:T(8,128)} %all-to-all-done, f32[102,16,96]{0,2,1:T(8,128)S(1)} %bitcast.51), kind=kOutput, calls=%fused_computation.49 | convolution fusion | flops 3128426496 | bytes 11476992 | tf_op jit(solution)/shard_map/rs,ksc->krc/dot_general | solution.py:138
  243.0 2.3 slice_subtract_fusion.2
  248.5 2.1 fusion.4
  (114 shorter events, 29.6 us)
Async XLA Ops:
  1.4 2.4 copy-start.6
  11.1 11.6 %copy-start.3 = (f32[12,96,128]{2,1,0:T(8,128)S(1)}, f32[12,96,128]{2,1,0:T(8,128)}, u32[]{:S(2)}) copy-start(f32[12,96,128]{2,1,0:T(8,128)} %param.12) | copy-start | bytes 1769476
  11.1 11.6 %copy-start.9 = (f32[12,96,128]{2,1,0:T(8,128)S(1)}, f32[12,96,128]{2,1,0:T(8,128)}, u32[]{:S(2)}) copy-start(f32[12,96,128]{2,1,0:T(8,128)} %param.13) | copy-start | bytes 1769476
  11.1 193.3 %all-to-all-start = ((f32[16,12,104,128]{3,2,1,0:T(8,128)}), f32[16,12,104,128]{3,2,1,0:T(8,128)}, u32[]{:S(2)}, u32[]{:S(2)}) async-start(f32[16,12,104,128]{3,2,1,0:T(8,128)} %stack.8), calls=%async_computation | async-start | bytes 20447232 | tf_op jit(solution)/shard_map/all_to_all | solution.py:119
  22.7 1.3 copy-start.21
  22.8 1.3 copy-start.19
  26.7 15.0 %copy-start.8 = (f32[96,1536]{1,0:T(8,128)S(1)}, f32[96,1536]{1,0:T(8,128)}, u32[]{:S(2)}) copy-start(f32[96,1536]{1,0:T(8,128)} %param.20) | copy-start | bytes 1769476
  28.9 147.6 %collective-permute-start.1 = (f32[39,96,3]{1,0,2:T(8,128)S(1)}, f32[39,96,3]{1,0,2:T(8,128)S(1)}, u32[]{:S(2)}, u32[]{:S(2)}) collective-permute-start(f32[39,96,3]{1,0,2:T(8,128)S(1)} %copy.22), channel_id=1, source_target_pairs={{16,0},{32,16},{48,32},{64,48},{80,64},{96,80},{112,96},{128,112},... | collective-permute-start | bytes 134792 | tf_op jit(solution)/shard_map/ppermute | solution.py:29
  39.7 138.6 %collective-permute-start = (f32[39,96,3]{1,0,2:T(8,128)S(1)}, f32[39,96,3]{1,0,2:T(8,128)S(1)}, u32[]{:S(2)}, u32[]{:S(2)}) collective-permute-start(f32[39,96,3]{1,0,2:T(8,128)S(1)} %copy.21), channel_id=1, source_target_pairs={{0,16},{16,32},{32,48},{48,64},{64,80},{80,96},{96,112},{112,128},... | collective-permute-start | bytes 134792 | tf_op jit(solution)/shard_map/ppermute | solution.py:28
  41.7 150.0 %collective-permute-start.5 = (f32[3,1536]{1,0:T(4,128)S(1)}, f32[3,1536]{1,0:T(4,128)S(1)}, u32[]{:S(2)}, u32[]{:S(2)}) collective-permute-start(f32[3,1536]{1,0:T(4,128)S(1)} %get-tuple-element.42), channel_id=1, source_target_pairs={{1,0},{2,1},{3,2},{4,3},{5,4},{6,5},{7,6},{8,7},{9,8},{10,9},{11,1... | collective-permute-start | bytes 55304 | tf_op jit(solution)/shard_map/ppermute | solution.py:40
  44.1 147.7 %collective-permute-start.4 = (f32[3,1536]{1,0:T(4,128)S(1)}, f32[3,1536]{1,0:T(4,128)S(1)}, u32[]{:S(2)}, u32[]{:S(2)}) collective-permute-start(f32[3,1536]{1,0:T(4,128)S(1)} %get-tuple-element.41), channel_id=1, source_target_pairs={{0,1},{1,2},{2,3},{3,4},{4,5},{5,6},{6,7},{7,8},{8,9},{9,10},{10,1... | collective-permute-start | bytes 55304 | tf_op jit(solution)/shard_map/ppermute | solution.py:39
  182.5 10.2 %collective-permute-start.3 = (f32[39,3,134]{2,1,0:T(4,128)}, f32[39,3,134]{2,1,0:T(4,128)S(1)}, u32[]{:S(2)}, u32[]{:S(2)}) collective-permute-start(f32[39,3,134]{2,1,0:T(4,128)} %get-tuple-element.23), channel_id=1, source_target_pairs={{1,0},{2,1},{3,2},{4,3},{5,4},{6,5},{7,6},{8,7},{9,8},{10,9},{11,1... | collective-permute-start | bytes 188144 | tf_op jit(solution)/shard_map/ppermute | solution.py:40
  185.0 9.0 %collective-permute-start.2 = (f32[39,3,134]{2,1,0:T(4,128)}, f32[39,3,134]{2,1,0:T(4,128)}, u32[]{:S(2)}, u32[]{:S(2)}) collective-permute-start(f32[39,3,134]{2,1,0:T(4,128)} %get-tuple-element.22), channel_id=1, source_target_pairs={{0,1},{1,2},{2,3},{3,4},{4,5},{5,6},{6,7},{7,8},{8,9},{9,10},{10,1... | collective-permute-start | bytes 188144 | tf_op jit(solution)/shard_map/ppermute | solution.py:39
  192.1 4.6 %copy-start.1 = (f32[39,96,3]{2,1,0:T(8,128)S(1)}, f32[39,96,3]{2,1,0:T(8,128)}, u32[]{:S(2)}) copy-start(f32[39,96,3]{2,1,0:T(8,128)} %copy.24) | copy-start | bytes 134788
  192.1 4.6 %copy-start.2 = (f32[39,96,3]{2,1,0:T(8,128)S(1)}, f32[39,96,3]{2,1,0:T(8,128)}, u32[]{:S(2)}) copy-start(f32[39,96,3]{2,1,0:T(8,128)} %copy.23) | copy-start | bytes 134788
  199.3 2.9 %copy-start = (f32[39,102,134]{2,1,0:T(8,128)}, f32[39,102,134]{2,1,0:T(8,128)S(1)}, u32[]{:S(2)}) copy-start(f32[39,102,134]{2,1,0:T(8,128)S(1)} %pad_maximum_fusion) | copy-start | bytes 6396628
  218.2 21.9 %collective-permute-start.7 = (f32[12,102,3]{1,0,2:T(8,128)S(1)}, f32[12,102,3]{1,0,2:T(8,128)}, u32[]{:S(2)}, u32[]{:S(2)}) collective-permute-start(f32[12,102,3]{1,0,2:T(8,128)S(1)} %get-tuple-element.62), channel_id=1, source_target_pairs={{16,0},{32,16},{48,32},{64,48},{80,64},{96,80},{112,96},{128,112},... | collective-permute-start | bytes 44072 | tf_op jit(solution)/shard_map/ppermute | solution.py:136
  228.3 12.8 %collective-permute-start.6 = (f32[12,102,3]{1,0,2:T(8,128)}, f32[12,102,3]{1,0,2:T(8,128)}, u32[]{:S(2)}, u32[]{:S(2)}) collective-permute-start(f32[12,102,3]{1,0,2:T(8,128)} %get-tuple-element.61), channel_id=1, source_target_pairs={{0,16},{16,32},{32,48},{48,64},{64,80},{80,96},{96,112},{112,128},... | collective-permute-start | bytes 44072 | tf_op jit(solution)/shard_map/ppermute | solution.py:135
  243.0 2.3 copy-start.13
  243.0 2.3 copy-start.14
  243.0 2.3 copy-start.32
  248.5 2.1 copy-start.12
  253.8 1.9 copy-start.30
  253.8 2.0 copy-start.7
  (18 other events, 19.1 us)
